TPU v7x, 256 devices: a whole 4x4x8 slice. The times are simulated.
256 devices in a mesh: dp: 2 (over z_lo), expert: 32 (over y, z_hi, core), tensor: 4 (over x).
Axes of the slice: x: 4, y: 4, z: 8 (z_hi: 4, z_lo: 2; z = z_hi * 2 + z_lo), core: 2. Of those that a mesh axis runs over, the one named last changes fastest.
Arguments:
- context: bfloat16 [8192, 2048], P(('dp', 'expert'), 'tensor'), may hold values from -6 to 6
- residual: bfloat16 [8192, 2048], P(('dp', 'expert')), may hold values from -6 to 6
- wo_rows: bfloat16 [2048, 2048], P('tensor'), may hold values from -0.125 to 0.125
- norm_gain: float32 [2048], replicated, may hold values from 0.25 to 1.75
- analyzer_out: bfloat16 [8192, 2048], P(('dp', 'expert'), 'tensor'), may hold values from -6 to 6
- gate_probs: float32 [8192, 6], P(('dp', 'expert')), may hold values from 0.05 to 0.5
- expert_ids: int32 [8192, 6], P(('dp', 'expert')), may hold values from 0 to 63, all different within a row; in each aligned block of 128 rows (0 to 127, 128 to 255, ...) at most 14 rows name the same one
- w_gate_up: bfloat16 [64, 2, 2048, 1408], P('expert', None, 'dp', 'tensor'), may hold values from -0.125 to 0.125
- w_down: bfloat16 [64, 1408, 2048], P('expert', 'tensor', 'dp'), may hold values from -0.15625 to 0.15625
Outputs:
- block_out: bfloat16 [8192, 2048], P(('dp', 'expert'), 'tensor')
- context_grad: bfloat16 [8192, 2048], P(('dp', 'expert'), 'tensor')
- gate_prob_grad: float32 [8192, 6], P(('dp', 'expert'))
- gate_up_grad: bfloat16 [64, 2, 2048, 1408], P('expert', None, 'dp', 'tensor')
- down_grad: bfloat16 [64, 1408, 2048], P('expert', 'tensor', 'dp')
Inputs may be any that keep to these rules, and one draw needn't show every extreme that they name: `expert_ids`: each row names 6 different experts; within each device's rows (aligned blocks of 128 rows) no expert is named more than 14 times, a bound that some block reaches.
All inputs are finite; a program needn't handle non-finite values.
Results may differ from a plain program's by a relative error of at most 0.024.
Values may be sent and summed in bfloat16 or wider, within the bound.
No kernel may reach another device: no remote copies, remote signals or barrier semaphores. Data moves between devices by JAX's collectives and lax.ppermute only.
A program may use at most 128 MiB of HBM per device.

v0:
```python
import jax
import jax.numpy as jnp
from jax import lax
from jax.sharding import PartitionSpec as P

EXPERTS = 64
CAP = 14
NORM_EPS = 1e-06
LOSS_WEIGHT = 0.25


def to_experts(outgoing):
    return lax.all_to_all(outgoing, "expert", split_axis=1, concat_axis=1, tiled=True)


def to_tokens(outgoing):
    return lax.all_to_all(outgoing, "expert", split_axis=1, concat_axis=1, tiled=True)


DP_SWAP = [(0, 1), (1, 0)]


def tensor_shift(value, shift, count):
    return lax.ppermute(value, "tensor", [(j, (j + shift) % count) for j in range(count)])


def by_source(received, count):
    order = (lax.axis_index("tensor") - jnp.arange(count)) % count
    return jnp.take(jnp.stack(received), order, axis=0)


def tensor_pieces(value):
    count = lax.axis_size("tensor")
    received = [value] + [tensor_shift(value, shift, count) for shift in range(1, count)]
    return by_source(received, count)


def tensor_total(value):
    pieces = tensor_pieces(value)
    total = pieces[0]
    for member in range(1, pieces.shape[0]):
        total = total + pieces[member]
    return total


def tensor_scattered(value):
    count = lax.axis_size("tensor")
    width = value.shape[1] // count
    me = lax.axis_index("tensor")
    received = [lax.dynamic_slice_in_dim(value, me * width, width, 1)]
    for shift in range(1, count):
        sent = lax.dynamic_slice_in_dim(value, (me + shift) % count * width, width, 1)
        received.append(tensor_shift(sent, shift, count))
    pieces = by_source(received, count).astype(jnp.float32)
    total = pieces[0]
    for member in range(1, count):
        total = total + pieces[member]
    return total


def dp_joined(own, dp_first, axis):
    other = lax.ppermute(own, "dp", DP_SWAP)
    return jnp.where(
        dp_first, jnp.concatenate([own, other], axis=axis), jnp.concatenate([other, own], axis=axis)
    )


def dp_halves_sent(part, dp_first, axis):
    half = part.shape[axis] // 2
    low = lax.slice_in_dim(part, 0, half, axis=axis).astype(jnp.bfloat16)
    high = lax.slice_in_dim(part, half, 2 * half, axis=axis).astype(jnp.bfloat16)
    kept = jnp.where(dp_first, low, high)
    arrived = lax.ppermute(jnp.where(dp_first, high, low), "dp", DP_SWAP)
    return (kept, arrived)


def halves_added(kept, arrived):
    return (kept.astype(jnp.float32) + arrived.astype(jnp.float32)).astype(jnp.bfloat16)


def weight_terms(arrived, activation, grad_in, d_gate_pre, d_up_pre):
    down_part = jnp.einsum(
        "escf,escd->efd", activation, grad_in, preferred_element_type=jnp.float32
    )
    gate_part = jnp.einsum(
        "escd,escf->edf", arrived, d_gate_pre, preferred_element_type=jnp.float32
    )
    up_part = jnp.einsum("escd,escf->edf", arrived, d_up_pre, preferred_element_type=jnp.float32)
    return (jnp.stack([gate_part, up_part], axis=1), down_part)


def per_device(
    context, residual, wo_rows, norm_gain, analyzer_out, gate_probs, expert_ids, w_gate_up, w_down
):
    tok_count, top_count = expert_ids.shape
    feature_count = residual.shape[1]
    tensor_count = lax.axis_size("tensor")
    expert_ranks = lax.axis_size("expert")
    col_count = feature_count // tensor_count
    col_start = lax.axis_index("tensor") * col_count
    local_experts = w_gate_up.shape[0]
    slot_count = EXPERTS * CAP
    expert_range = jnp.arange(EXPERTS, dtype=jnp.int32)
    slot_order = expert_range % local_experts * expert_ranks + expert_range // local_experts
    dp_first = lax.axis_index("dp") == 0
    down_other = lax.ppermute(w_down, "dp", DP_SWAP)
    partial_attn = jnp.dot(context, wo_rows, preferred_element_type=jnp.float32)
    attn_cols = tensor_scattered(partial_attn.astype(jnp.bfloat16))
    hidden_cols = (
        lax.dynamic_slice_in_dim(residual, col_start, col_count, 1).astype(jnp.float32) + attn_cols
    )
    square_sum = tensor_total(jnp.sum(hidden_cols * hidden_cols, axis=1, keepdims=True))
    inv_rms = lax.rsqrt(square_sum / feature_count + NORM_EPS)
    gain_cols = lax.dynamic_slice_in_dim(norm_gain, col_start, col_count, 0)
    normed = (gain_cols * hidden_cols * inv_rms).astype(jnp.bfloat16)
    flat_ids = expert_ids.reshape(-1)
    onehot = (flat_ids[:, None] == expert_range[None, :]).astype(jnp.int32)
    slot_index = jnp.sum((jnp.cumsum(onehot, axis=0) - onehot) * onehot, axis=1)
    expert_slot = jnp.sum(onehot * slot_order[None, :], axis=1)
    dest_row = expert_slot * CAP + slot_index
    sentinel = tok_count * top_count
    row_entry = (
        jnp.full((slot_count,), sentinel, jnp.int32)
        .at[dest_row]
        .set(jnp.arange(sentinel, dtype=jnp.int32))
    )
    row_token = row_entry // top_count
    gate_pad = jnp.concatenate([gate_probs.reshape(-1), jnp.zeros((1,), jnp.float32)])
    row_gate = gate_pad[row_entry]
    normed_pad = jnp.concatenate([normed, jnp.zeros((1, col_count), jnp.bfloat16)], axis=0)
    outgoing = normed_pad[row_token].reshape(local_experts, expert_ranks, CAP, col_count)
    first_other = lax.ppermute(w_gate_up[0:1, 0:1], "dp", DP_SWAP)
    down_other, first_other, outgoing = lax.optimization_barrier(
        (down_other, first_other, outgoing)
    )
    second_other = lax.ppermute(w_gate_up[0:1, 1:2], "dp", DP_SWAP)
    rest_other = lax.ppermute(w_gate_up[1:], "dp", DP_SWAP)
    gate_up_other = jnp.concatenate(
        [jnp.concatenate([first_other, second_other], axis=1), rest_other], axis=0
    )
    gate_up_full = jnp.where(
        dp_first,
        jnp.concatenate([w_gate_up, gate_up_other], axis=2),
        jnp.concatenate([gate_up_other, w_gate_up], axis=2),
    )
    down_full = jnp.where(
        dp_first,
        jnp.concatenate([w_down, down_other], axis=2),
        jnp.concatenate([down_other, w_down], axis=2),
    )
    arrived = lax.all_gather(to_experts(outgoing), "tensor", axis=3, tiled=True)
    gate_full = gate_up_full[:, 0]
    up_full = gate_up_full[:, 1]
    half_count = feature_count // 2
    dp_index = lax.axis_index("dp")
    own_rows = lax.dynamic_slice_in_dim(arrived, dp_index * half_count, half_count, 3)
    other_rows = lax.dynamic_slice_in_dim(arrived, (1 - dp_index) * half_count, half_count, 3)
    other_pieces = ((first_other[0, 0], second_other[0, 0]), (rest_other[0, 0], rest_other[0, 1]))

    def projected(which):
        return jnp.stack(
            [
                jnp.einsum(
                    "scd,df->scf",
                    own_rows[e],
                    w_gate_up[e, which],
                    preferred_element_type=jnp.float32,
                )
                + jnp.einsum(
                    "scd,df->scf",
                    other_rows[e],
                    other_pieces[e][which],
                    preferred_element_type=jnp.float32,
                )
                for e in range(local_experts)
            ]
        )

    pre_gate = projected(0)
    pre_up = projected(1)
    activation = (jax.nn.silu(pre_gate) * pre_up).astype(jnp.bfloat16)
    partial_out = jnp.einsum(
        "escf,efd->escd", activation, down_full, preferred_element_type=jnp.float32
    )
    summed_out = lax.psum_scatter(
        partial_out.astype(jnp.bfloat16), "tensor", scatter_dimension=3, tiled=True
    )
    returned = to_tokens(summed_out).reshape(slot_count, col_count)
    entry_out = returned[dest_row].reshape(tok_count, top_count, col_count).astype(jnp.float32)
    block_out = (hidden_cols + jnp.sum(gate_probs[:, :, None] * entry_out, axis=1)).astype(
        jnp.bfloat16
    )
    error = (
        LOSS_WEIGHT * (block_out.astype(jnp.float32) - analyzer_out.astype(jnp.float32))
    ).astype(jnp.bfloat16)
    gate_partial = jnp.sum(error.astype(jnp.float32)[:, None, :] * entry_out, axis=2)
    error_pad = jnp.concatenate([error, jnp.zeros((1, col_count), jnp.bfloat16)], axis=0)
    grad_slot = (row_gate[:, None] * error_pad[row_token].astype(jnp.float32)).astype(jnp.bfloat16)
    grad_slot = grad_slot.reshape(local_experts, expert_ranks, CAP, col_count)
    grad_in = lax.all_gather(to_experts(grad_slot), "tensor", axis=3, tiled=True)
    d_act = jnp.einsum("escd,efd->escf", grad_in, down_full, preferred_element_type=jnp.float32)
    sigmoid_pre = jax.nn.sigmoid(pre_gate)
    d_gate_pre = (d_act * pre_up * sigmoid_pre * (1.0 + pre_gate * (1.0 - sigmoid_pre))).astype(
        jnp.bfloat16
    )
    d_up_pre = (d_act * pre_gate * sigmoid_pre).astype(jnp.bfloat16)
    d_entry_part = jnp.einsum(
        "escf,edf->escd", d_gate_pre, gate_full, preferred_element_type=jnp.float32
    )
    d_entry_part = d_entry_part + jnp.einsum(
        "escf,edf->escd", d_up_pre, up_full, preferred_element_type=jnp.float32
    )
    d_entry_sum = lax.psum_scatter(
        d_entry_part.astype(jnp.bfloat16), "tensor", scatter_dimension=3, tiled=True
    )
    d_returned = to_tokens(d_entry_sum).reshape(slot_count, col_count)
    d_normed = jnp.sum(
        d_returned[dest_row].reshape(tok_count, top_count, col_count).astype(jnp.float32), axis=1
    )
    scaled = gain_cols * d_normed
    norm_partial = jnp.sum(scaled * hidden_cols, axis=1)
    norm_dots, gate_prob_grad = lax.psum((norm_partial, gate_partial), "tensor")
    cubed = inv_rms * inv_rms * inv_rms
    d_hidden = (
        error.astype(jnp.float32)
        + inv_rms * scaled
        - hidden_cols * cubed * norm_dots[:, None] / feature_count
    ).astype(jnp.bfloat16)
    context_grad = lax.dot_general(
        lax.all_gather(d_hidden, "tensor", axis=1, tiled=True),
        wo_rows,
        (((1,), (1,)), ((), ())),
        preferred_element_type=jnp.float32,
    ).astype(jnp.bfloat16)
    gate_up_part, down_part = weight_terms(arrived, activation, grad_in, d_gate_pre, d_up_pre)
    gate_up_kept, gate_up_arrived = dp_halves_sent(gate_up_part, dp_first, 2)
    down_kept, down_arrived = dp_halves_sent(down_part, dp_first, 2)
    gate_up_arrived, down_arrived, context_grad = lax.optimization_barrier(
        (gate_up_arrived, down_arrived, context_grad)
    )
    return (
        block_out,
        context_grad,
        gate_prob_grad,
        halves_added(gate_up_kept, gate_up_arrived),
        halves_added(down_kept, down_arrived),
    )


def solution(mesh):
    in_specs = (
        P(("dp", "expert"), "tensor"),
        P(("dp", "expert"), None),
        P("tensor", None),
        P(),
        P(("dp", "expert"), "tensor"),
        P(("dp", "expert"), None),
        P(("dp", "expert"), None),
        P("expert", None, "dp", "tensor"),
        P("expert", "tensor", "dp"),
    )
    out_specs = (
        P(("dp", "expert"), "tensor"),
        P(("dp", "expert"), "tensor"),
        P(("dp", "expert"), None),
        P("expert", None, "dp", "tensor"),
        P("expert", "tensor", "dp"),
    )
    return jax.shard_map(
        per_device, mesh=mesh, in_specs=in_specs, out_specs=out_specs, check_vma=False
    )
```

profile of v0, /device:TPU:32, one launch (start us, length us, event | category | flops | bytes accessed | tf_op | source)
XLA Modules:
  0.0 521.8 jit_solution(2365264565536121640)
XLA Ops:
  12.5 2.7 collective-permute-start.1
  22.7 3.4 scatter_custom_fusion
  37.5 4.0 gather_fusion.2
  43.6 22.6 %collective-permute-done.3 = bf16[2,352,1024]{2,1,0:T(8,128)(2,1)} collective-permute-done((bf16[2,352,1024]{2,1,0:T(8,128)(2,1)}, bf16[2,352,1024]{2,1,0:T(8,128)(2,1)}, u32[]{:S(2)}, u32[]{:S(2)}) %collective-permute-start.3) | collective-permute-done | bytes 1441824 | tf_op jit(solution)/shard_map/ppermute | solution.py:106
  68.3 36.9 %all_to_all.20 = bf16[2,32,14,512]{3,0,2,1:T(2,128)(2,1)S(1)} all-to-all(bf16[2,32,14,512]{3,0,2,1:T(2,128)(2,1)S(1)} %copy.62), channel_id=1, replica_groups=mesh['dp'=2,'expert'=32,'tensor'=4] {'expert'}, dimensions={1} | all-to-all | bytes 1835008 | tf_op jit(solution)/shard_map/all_to_all | solution.py:13
  106.4 2.6 slice.107
  111.2 36.1 %all-gather.3.cloned.1.call-done = bf16[2,32,14,2048]{3,1,2,0:T(8,128)(2,1)} async-done(((bf16[2,32,14,512]{3,1,2,0:T(8,128)(2,1)}), bf16[2,32,14,2048]{3,1,2,0:T(8,128)(2,1)}) %all-gather.3.cloned.1.call-update) | async-done | bytes 3670032 | tf_op jit(solution)/shard_map/all_gather | solution.py:151
  162.5 7.0 %convolution_convert_fusion = bf16[2,32,14,2048]{3,1,2,0:T(8,128)(2,1)} fusion(bf16[2,32,14,352]{3,1,2,0:T(8,128)(2,1)S(1)} %multiply_convert_fusion.3, bf16[2,352,1024]{2,1,0:T(8,128)(2,1)} %collective-permute-done.3, bf16[2,352,1024]{2,1,0:T(8,128)(2,1)} %param.17, pred[]{:T(512)S(6)} %eq.45), kind=kOutput, calls=%fused_computation.15 | convolution fusion | flops 1306656768 | bytes 7184385 | tf_op jit(solution)/shard_map/escf,efd->escd/dot_general | solution.py:182
  169.5 45.5 %reduce-scatter.3.cloned.1.call-done = bf16[2,32,14,512]{3,1,2,0:T(8,128)(2,1)} async-done(((bf16[2,32,14,2048]{3,1,2,0:T(8,128)(2,1)}), bf16[2,32,14,512]{3,1,2,0:T(8,128)(2,1)}) %reduce-scatter.3.cloned.1.call-update) | async-done | bytes 917520 | tf_op jit(solution)/shard_map/reduce_scatter | solution.py:185
  215.1 3.0 copy.64
  218.1 9.1 %all-to-all-start.1 = ((bf16[2,32,14,512]{3,0,2,1:T(2,128)(2,1)}), bf16[2,32,14,512]{3,0,2,1:T(2,128)(2,1)}, u32[]{:S(2)}, u32[]{:S(2)}) async-start(bf16[2,32,14,512]{3,0,2,1:T(2,128)(2,1)} %copy.64), calls=%async_computation.2 | async-start | bytes 1835008 | tf_op jit(solution)/shard_map/all_to_all | solution.py:17
  227.7 3.7 gather_fusion.4
  231.5 19.0 %all-to-all-done.1 = bf16[2,32,14,512]{3,0,2,1:T(2,128)(2,1)} async-done(((bf16[2,32,14,512]{3,0,2,1:T(2,128)(2,1)}), bf16[2,32,14,512]{3,0,2,1:T(2,128)(2,1)}, u32[]{:S(2)}, u32[]{:S(2)}) %all-to-all-start.1) | async-done | bytes 917536 | tf_op jit(solution)/shard_map/all_to_all | solution.py:17
  254.3 3.3 gather_fusion.3
  263.3 4.0 gather_fusion.5
  272.5 30.2 %all_to_all.21 = bf16[2,32,14,512]{3,0,2,1:T(2,128)(2,1)S(1)} all-to-all(bf16[2,32,14,512]{3,0,2,1:T(2,128)(2,1)S(1)} %copy.67), channel_id=1, replica_groups=mesh['dp'=2,'expert'=32,'tensor'=4] {'expert'}, dimensions={1} | all-to-all | bytes 1835008 | tf_op jit(solution)/shard_map/all_to_all | solution.py:13
  304.2 7.6 %maximum_select_fusion = bf16[2,2,2048,352]{2,3,1,0:T(8,128)(2,1)} fusion(bf16[1,2,1024,352]{2,3,1,0:T(8,128)(2,1)} %collective-permute-done.8, bf16[1,1,1024,352]{2,3,1,0:T(8,128)(2,1)} %collective-permute-done.9, bf16[1,1,1024,352]{2,3,1,0:T(8,128)(2,1)S(1)} %copy-done.11, bf16[2,2,1024,352]{2,3,1,0:T(8,128)(2,1)} %param.16, pred[]{:T(512)S(6)} %eq.45), kind=kLoop, calls=%fused_computation.10 | loop fusion | flops 49020928 | bytes 11534337 | tf_op jit(solution)/shard_map/jit(_where)/select_n | solution.py:141
  311.8 38.6 %all-gather.5.cloned.1.call-done = bf16[2,32,14,2048]{3,1,2,0:T(8,128)(2,1)} async-done(((bf16[2,32,14,512]{3,1,2,0:T(8,128)(2,1)}), bf16[2,32,14,2048]{3,1,2,0:T(8,128)(2,1)}) %all-gather.5.cloned.1.call-update) | async-done | bytes 3670032 | tf_op jit(solution)/shard_map/all_gather | solution.py:200
  350.3 7.0 %multiply_convert_fusion.2 = (bf16[2,32,14,352]{3,1,2,0:T(8,128)(2,1)S(1)}, bf16[2,32,14,352]{3,1,2,0:T(8,128)(2,1)S(1)}) fusion(f32[1,32,14,352]{3,1,2,0:T(8,128)} %copy-done.14, f32[1,32,14,352]{3,1,2,0:T(8,128)} %copy-done.15, f32[1,32,14,352]{3,1,2,0:T(8,128)} %copy-done.13, f32[1,32,14,352]{3,1,2,0:T(8,128)} %copy-done.12, ...), kind=kOutput, calls=%fused_computation.32 | convolution fusion | flops 1309552640 | bytes 10338305 | tf_op jit(solution)/shard_map/escd,efd->escf/dot_general | solution.py:201
  359.5 3.9 add_convert_fusion
  363.5 3.9 convolution_bitcast_fusion.1
  373.6 35.4 %reduce-scatter.5.cloned.1.call-done = bf16[2,32,14,512]{3,1,2,0:T(8,128)(2,1)} async-done(((bf16[2,32,14,2048]{3,1,2,0:T(8,128)(2,1)}), bf16[2,32,14,512]{3,1,2,0:T(8,128)(2,1)}) %reduce-scatter.5.cloned.1.call-update) | async-done | bytes 917520 | tf_op jit(solution)/shard_map/reduce_scatter | solution.py:213
  409.0 3.1 copy.69
  412.1 8.9 %all-to-all-start.3 = ((bf16[2,32,14,512]{3,0,2,1:T(2,128)(2,1)}), bf16[2,32,14,512]{3,0,2,1:T(2,128)(2,1)S(1)}, u32[]{:S(2)}, u32[]{:S(2)}) async-start(bf16[2,32,14,512]{3,0,2,1:T(2,128)(2,1)} %copy.69), calls=%async_computation.5 | async-start | bytes 1835008 | tf_op jit(solution)/shard_map/all_to_all | solution.py:17
  421.0 4.0 bitcast_convert_fusion
  429.6 31.2 %all-to-all-done.3 = bf16[2,32,14,512]{3,0,2,1:T(2,128)(2,1)S(1)} async-done(((bf16[2,32,14,512]{3,0,2,1:T(2,128)(2,1)}), bf16[2,32,14,512]{3,0,2,1:T(2,128)(2,1)S(1)}, u32[]{:S(2)}, u32[]{:S(2)}) %all-to-all-start.3) | async-done | bytes 917536 | tf_op jit(solution)/shard_map/all_to_all | solution.py:17
  463.4 3.3 gather_fusion.6
  466.7 2.6 reshape.264
  471.6 16.2 %all-reduce.2 = (f32[128]{0:T(128)S(1)}, f32[128,6]{1,0:T(8,128)S(1)}) all-reduce(f32[128]{0:T(128)S(1)} %multiply_reduce_fusion.2, f32[128,6]{1,0:T(8,128)S(1)} %multiply_reduce_fusion), channel_id=1, replica_groups=mesh['dp'=2,'expert'=32,'tensor'=4] {'tensor'}, use_global_device_ids=true, to_apply=%region_11.12 | all-reduce | flops 896 | bytes 7168 | tf_op jit(solution)/shard_map/psum | solution.py:222
  488.0 13.6 %all_gather.11 = bf16[128,2048]{1,0:T(8,128)(2,1)S(1)} all-gather(bf16[128,512]{1,0:T(8,128)(2,1)S(1)} %subtract_convert_fusion), channel_id=1, replica_groups=mesh['dp'=2,'expert'=32,'tensor'=4] {'tensor'}, dimensions={1}, use_global_device_ids=true | all-gather | bytes 655360 | tf_op jit(solution)/shard_map/all_gather | solution.py:230
  503.1 3.4 add_convert_fusion.2
  506.5 5.7 %add_convert_fusion.1 = bf16[2,2,1024,352]{2,3,0,1:T(8,128)(2,1)S(1)} fusion(bf16[2,2,1024,352]{2,3,0,1:T(8,128)(2,1)} %collective-permute-done.10, pred[]{:T(512)S(6)} %eq.45, bf16[2,2,2048,352]{2,3,0,1:T(8,128)(2,1)} %copy-done.1), kind=kLoop, calls=%fused_computation.12 | loop fusion | flops 7208960 | bytes 11534337 | tf_op jit(solution)/shard_map/convert_element_type | solution.py:78
  (148 shorter events, 85.5 us)
Async XLA Ops:
  7.2 140.1 %all-gather.3.cloned.1.call-start = ((), (), s32[]{:S(2)}) async-start(), calls=%async_computation.6 | async-start | bytes 4587520 | tf_op jit(solution)/shard_map/all_gather | solution.py:151
  8.8 7.9 %copy-start.6 = (bf16[2,2,1024,352]{2,3,1,0:T(8,128)(2,1)S(1)}, bf16[2,2,1024,352]{2,3,1,0:T(8,128)(2,1)}, u32[]{:S(2)}) copy-start(bf16[2,2,1024,352]{2,3,1,0:T(8,128)(2,1)} %param.16) | copy-start | bytes 8650756
  8.8 11.2 %copy-start.21 = (s32[128,6]{0,1:T(8,128)S(1)}, s32[128,6]{0,1:T(8,128)}, u32[]{:S(2)}) copy-start(s32[128,6]{0,1:T(8,128)} %param.15) | copy-start | bytes 9220
  11.0 15.1 %collective-permute-start = (bf16[128,512]{1,0:T(8,128)(2,1)}, bf16[128,512]{1,0:T(8,128)(2,1)}, u32[]{:S(2)}, u32[]{:S(2)}) collective-permute-start(bf16[128,512]{1,0:T(8,128)(2,1)} %get-tuple-element.55), channel_id=1, source_target_pairs={{0,1},{1,2},{2,3},{3,0},{4,5},{5,6},{6,7},{7,4},{8,9},{9,10},{10,1... | collective-permute-start | bytes 393224 | tf_op jit(solution)/shard_map/ppermute | solution.py:24
  12.5 13.6 %collective-permute-start.1 = (bf16[128,512]{1,0:T(8,128)(2,1)}, bf16[128,512]{1,0:T(8,128)(2,1)}, u32[]{:S(2)}, u32[]{:S(2)}) collective-permute-start(bf16[128,512]{1,0:T(8,128)(2,1)} %get-tuple-element.54), channel_id=1, source_target_pairs={{0,2},{1,3},{2,0},{3,1},{4,6},{5,7},{6,4},{7,5},{8,10},{9,11},{10,... | collective-permute-start | bytes 393224 | tf_op jit(solution)/shard_map/ppermute | solution.py:24
  15.3 10.9 %collective-permute-start.2 = (bf16[128,512]{1,0:T(8,128)(2,1)S(1)}, bf16[128,512]{1,0:T(8,128)(2,1)}, u32[]{:S(2)}, u32[]{:S(2)}) collective-permute-start(bf16[128,512]{1,0:T(8,128)(2,1)S(1)} %get-tuple-element.53), channel_id=1, source_target_pairs={{0,3},{1,0},{2,1},{3,2},{4,7},{5,4},{6,5},{7,6},{8,11},{9,8},{10,9... | collective-permute-start | bytes 393224 | tf_op jit(solution)/shard_map/ppermute | solution.py:24
  17.9 25.7 %collective-permute-start.4 = (bf16[1,1,1024,352]{2,3,1,0:T(8,128)(2,1)}, bf16[1,1,1024,352]{2,3,1,0:T(8,128)(2,1)S(1)}, u32[]{:S(2)}, u32[]{:S(2)}) collective-permute-start(bf16[1,1,1024,352]{2,3,1,0:T(8,128)(2,1)} %get-tuple-element.49), channel_id=1, source_target_pairs={{0,128},{128,0},{1,129},{129,1},{2,130},{130,2},{3,131},{131,3},{4... | collective-permute-start | bytes 2162696 | tf_op jit(solution)/shard_map/ppermute | solution.py:132
  18.0 48.1 %collective-permute-start.3 = (bf16[2,352,1024]{2,1,0:T(8,128)(2,1)}, bf16[2,352,1024]{2,1,0:T(8,128)(2,1)}, u32[]{:S(2)}, u32[]{:S(2)}) collective-permute-start(bf16[2,352,1024]{2,1,0:T(8,128)(2,1)} %param.17), channel_id=1, source_target_pairs={{0,128},{128,0},{1,129},{129,1},{2,130},{130,2},{3,131},{131,3},{4... | collective-permute-start | bytes 4325384 | tf_op jit(solution)/shard_map/ppermute | solution.py:106
  31.0 4.8 collective-permute-start.5
  31.6 5.1 collective-permute-start.6
  32.5 4.2 collective-permute-start.7
  43.6 105.8 %copy-start.10 = (bf16[1,1,1024,352]{2,3,1,0:T(8,128)(2,1)}, bf16[1,1,1024,352]{2,3,1,0:T(8,128)(2,1)S(1)}, u32[]{:S(2)}) copy-start(bf16[1,1,1024,352]{2,3,1,0:T(8,128)(2,1)S(1)} %collective-permute-done.4) | copy-start | bytes 2162692
  106.4 108.7 %reduce-scatter.3.cloned.1.call-start = ((), (), s32[]{:S(2)}) async-start(), calls=%async_computation.7 | async-start | bytes 4587520 | tf_op jit(solution)/shard_map/reduce_scatter | solution.py:185
  109.0 44.6 %collective-permute-start.8 = (bf16[1,2,1024,352]{2,3,1,0:T(8,128)(2,1)}, bf16[1,2,1024,352]{2,3,1,0:T(8,128)(2,1)}, u32[]{:S(2)}, u32[]{:S(2)}) collective-permute-start(bf16[1,2,1024,352]{2,3,1,0:T(8,128)(2,1)} %slice.107), channel_id=1, source_target_pairs={{0,128},{128,0},{1,129},{129,1},{2,130},{130,2},{3,131},{131,3},{4... | collective-permute-start | bytes 4325384 | tf_op jit(solution)/shard_map/ppermute | solution.py:137
  109.9 48.6 %collective-permute-start.9 = (bf16[1,1,1024,352]{2,3,1,0:T(8,128)(2,1)}, bf16[1,1,1024,352]{2,3,1,0:T(8,128)(2,1)}, u32[]{:S(2)}, u32[]{:S(2)}) collective-permute-start(bf16[1,1,1024,352]{2,3,1,0:T(8,128)(2,1)} %get-tuple-element.48), channel_id=1, source_target_pairs={{0,128},{128,0},{1,129},{129,1},{2,130},{130,2},{3,131},{131,3},{4... | collective-permute-start | bytes 2162696 | tf_op jit(solution)/shard_map/ppermute | solution.py:136
  147.3 4.2 copy-start.7
  149.5 4.1 copy-start.8
  151.5 8.8 %copy-start.12 = (f32[1,32,14,352]{3,1,2,0:T(8,128)}, f32[1,32,14,352]{3,1,2,0:T(8,128)S(1)}, u32[]{:S(2)}) copy-start(f32[1,32,14,352]{3,1,2,0:T(8,128)S(1)} %fusion.8) | copy-start | bytes 1892356
  155.4 4.9 copy-start.13
  169.5 57.9 %copy-start.22 = (f32[128,6]{0,1:T(8,128)S(1)}, f32[128,6]{0,1:T(8,128)}, u32[]{:S(2)}) copy-start(f32[128,6]{0,1:T(8,128)} %param.14) | copy-start | bytes 9220
  218.1 32.4 %all-to-all-start.1 = ((bf16[2,32,14,512]{3,0,2,1:T(2,128)(2,1)}), bf16[2,32,14,512]{3,0,2,1:T(2,128)(2,1)}, u32[]{:S(2)}, u32[]{:S(2)}) async-start(bf16[2,32,14,512]{3,0,2,1:T(2,128)(2,1)} %copy.64), calls=%async_computation.2 | async-start | bytes 1835008 | tf_op jit(solution)/shard_map/all_to_all | solution.py:17
  227.2 123.2 %all-gather.5.cloned.1.call-start = ((), (), s32[]{:S(2)}) async-start(), calls=%async_computation.8 | async-start | bytes 4587520 | tf_op jit(solution)/shard_map/all_gather | solution.py:200
  257.6 4.8 copy-start.20
  271.6 32.7 %copy-start.11 = (bf16[1,1,1024,352]{2,3,1,0:T(8,128)(2,1)S(1)}, bf16[1,1,1024,352]{2,3,1,0:T(8,128)(2,1)}, u32[]{:S(2)}) copy-start(bf16[1,1,1024,352]{2,3,1,0:T(8,128)(2,1)} %copy-done.10) | copy-start | bytes 2162692
  303.9 105.1 %reduce-scatter.5.cloned.1.call-start = ((), (), s32[]{:S(2)}) async-start(), calls=%async_computation.9 | async-start | bytes 4587520 | tf_op jit(solution)/shard_map/reduce_scatter | solution.py:213
  350.3 7.1 %copy-start.2 = (bf16[2,2,2048,352]{2,3,1,0:T(8,128)(2,1)S(1)}, bf16[2,2,2048,352]{2,3,1,0:T(8,128)(2,1)}, u32[]{:S(2)}) copy-start(bf16[2,2,2048,352]{2,3,1,0:T(8,128)(2,1)} %maximum_select_fusion) | copy-start | bytes 17301508
  363.5 3.9 copy-start.9
  363.5 3.9 copy-start.19
  373.1 130.0 %collective-permute-start.10 = (bf16[2,2,1024,352]{2,3,0,1:T(8,128)(2,1)}, bf16[2,2,1024,352]{2,3,0,1:T(8,128)(2,1)}, u32[]{:S(2)}, u32[]{:S(2)}) collective-permute-start(bf16[2,2,1024,352]{2,3,0,1:T(8,128)(2,1)} %broadcast_select_fusion), channel_id=1, source_target_pairs={{0,128},{128,0},{1,129},{129,1},{2,130},{130,2},{3,131},{131,3},{4... | collective-permute-start | bytes 8650760 | tf_op jit(solution)/shard_map/ppermute | solution.py:73
  412.1 48.7 %all-to-all-start.3 = ((bf16[2,32,14,512]{3,0,2,1:T(2,128)(2,1)}), bf16[2,32,14,512]{3,0,2,1:T(2,128)(2,1)S(1)}, u32[]{:S(2)}, u32[]{:S(2)}) async-start(bf16[2,32,14,512]{3,0,2,1:T(2,128)(2,1)} %copy.69), calls=%async_computation.5 | async-start | bytes 1835008 | tf_op jit(solution)/shard_map/all_to_all | solution.py:17
  427.8 75.2 %collective-permute-start.11 = (bf16[2,352,1024]{2,1,0:T(8,128)(2,1)}, bf16[2,352,1024]{2,1,0:T(8,128)(2,1)}, u32[]{:S(2)}, u32[]{:S(2)}) collective-permute-start(bf16[2,352,1024]{2,1,0:T(8,128)(2,1)} %broadcast_select_fusion.1), channel_id=1, source_target_pairs={{0,128},{128,0},{1,129},{129,1},{2,130},{130,2},{3,131},{131,3},{4... | collective-permute-start | bytes 4325384 | tf_op jit(solution)/shard_map/ppermute | solution.py:73
  487.8 15.2 %copy-start.5 = (bf16[2,352,2048]{2,1,0:T(8,128)(2,1)S(1)}, bf16[2,352,2048]{2,1,0:T(8,128)(2,1)}, u32[]{:S(2)}) copy-start(bf16[2,352,2048]{2,1,0:T(8,128)(2,1)} %copy-done.4) | copy-start | bytes 8650756
  (9 other events, 18.2 us)
Sparse Core Ops, SparseCore 0:
  106.5 40.7 all-gather.2
  169.6 45.3 reduce-scatter.2
  304.0 46.2 all-gather.4
  363.6 45.3 reduce-scatter.4
where the time goes:
time: 531 us; the launch traced here: 522 us
  waiting for transfers between devices  230 us (43%)
  blocking collectives  96.9 us (18%)
  local copies, waits for them, and re-layouts  66.3 us (12%)
  matrix products  45.5 us (9%)
  other arithmetic  34.5 us (6%)
  starting transfers between devices  33.8 us (6%)
  between operations  14.9 us (3%)
    all_to_all x2, blocking collectives, to_experts(): lax.all_to_all(outgoing, 'expert', split_axis=1, concat_axis=1, tiled=True)  67.1 us
    all_to_all x2, waiting for transfers between devices, to_tokens(): lax.all_to_all(outgoing, 'expert', split_axis=1, concat_axis=1, tiled=True)  50.2 us
    reduce_scatter x1, waiting for transfers between devices, per_device(): lax.psum_scatter(partial_out.astype(jnp.bfloat16), 'tensor', scatter_dime...  45.5 us
    all_gather x1, waiting for transfers between devices, per_device(): lax.all_gather(to_experts(grad_slot), 'tensor', axis=3, tiled=True)  38.6 us
    all_gather x1, waiting for transfers between devices, per_device(): arrived = lax.all_gather(to_experts(outgoing), 'tensor', axis=3, tiled=True)  36.1 us
    reduce_scatter x1, waiting for transfers between devices, per_device(): lax.psum_scatter(d_entry_part.astype(jnp.bfloat16), 'tensor', scatter_dim...  35.4 us
    ppermute x1, waiting for transfers between devices, per_device(): down_other = lax.ppermute(w_down, 'dp', DP_SWAP)  22.6 us
    all_to_all x2, starting transfers between devices, to_tokens(): lax.all_to_all(outgoing, 'expert', split_axis=1, concat_axis=1, tiled=True)  18 us
  transfers between devices with their start and end apart: 18, of which 9 were waited for; matrix products, arithmetic and copies ran while one was open for 14% of the time, Pallas kernels for 0%

commit v1 on v0

--- a/solution.py
+++ b/solution.py
@@ -7,6 +7,28 @@
 CAP = 14
 NORM_EPS = 1e-06
 LOSS_WEIGHT = 0.25
+
+
+def joined_along(parts, dim):
+    shape = list(parts.shape[1:])
+    shape[dim] *= parts.shape[0]
+    return jnp.moveaxis(parts, 0, dim).reshape(shape)
+
+
+def gather_around(value, axis, dim):
+    size = lax.axis_size(axis)
+    pairs = [(i, (i + 1) % size) for i in range(size)]
+    back = [(b, a) for a, b in pairs]
+    lower, upper = ([], [])
+    for step in range(size - 1):
+        if step % 2 == 0:
+            lower.append(lax.ppermute(lower[-1] if lower else value, axis, pairs))
+        else:
+            upper.append(lax.ppermute(upper[-1] if upper else value, axis, back))
+    blocks = jnp.stack([*lower[::-1], value, *upper])
+    shift = lax.axis_index(axis) - len(lower)
+    blocks = blocks[(jnp.arange(size) - shift) % size]
+    return joined_along(blocks, dim)
 
 
 def to_experts(outgoing):
@@ -197,7 +219,7 @@
     error_pad = jnp.concatenate([error, jnp.zeros((1, col_count), jnp.bfloat16)], axis=0)
     grad_slot = (row_gate[:, None] * error_pad[row_token].astype(jnp.float32)).astype(jnp.bfloat16)
     grad_slot = grad_slot.reshape(local_experts, expert_ranks, CAP, col_count)
-    grad_in = lax.all_gather(to_experts(grad_slot), "tensor", axis=3, tiled=True)
+    grad_in = gather_around(to_experts(grad_slot), "tensor", 3)
     d_act = jnp.einsum("escd,efd->escf", grad_in, down_full, preferred_element_type=jnp.float32)
     sigmoid_pre = jax.nn.sigmoid(pre_gate)
     d_gate_pre = (d_act * pre_up * sigmoid_pre * (1.0 + pre_gate * (1.0 - sigmoid_pre))).astype(

time: 531 us -> 571 us (1.075)
  local copies, waits for them, and re-layouts: 66.3 us -> 96.5 us
  waiting for transfers between devices: 230 us -> 219 us
  starting transfers between devices: 33.8 us -> 42.5 us
  other arithmetic: 34.5 us -> 42.4 us
    all_gather x1 -> x0, waiting for transfers between devices: 38.6 us -> none  [per_device(): lax.all_gather(to_experts(grad_slot), 'tensor', axis=3, tiled=True)]
    ppermute x0 -> x3, waiting for transfers between devices: none -> 32.8 us  [the longest x2 32.8 us: gather_around(): lower.append(lax.ppermute(lower[-1] if lower else value, axis, pairs))]
    gather x0 -> x1, local copies, waits for them, and re-layouts: none -> 11.2 us  [gather_around(): blocks = blocks[(jnp.arange(size) - shift) % size]]
    reduce_scatter x1, waiting for transfers between devices: 35.4 us -> 26.8 us  [per_device(): lax.psum_scatter(d_entry_part.astype(jnp.bfloat16), 'tensor', scatter_dim...]
    another operation x3 -> x4, other arithmetic: 2.35 us -> 9.97 us  [the longest x1 7.62 us: gather_around(): blocks = jnp.stack([*lower[::-1], value, *upper])]
    reshape x0 -> x1, local copies, waits for them, and re-layouts: none -> 7.36 us  [joined_along(): return jnp.moveaxis(parts, 0, dim).reshape(shape)]
    transpose x0 -> x1, local copies, waits for them, and re-layouts: none -> 6.64 us  [joined_along(): return jnp.moveaxis(parts, 0, dim).reshape(shape)]
  transfers between devices with their start and end apart: 18 -> 20, of which waited for: 9 -> 10; matrix products, arithmetic and copies ran while one was open for 14% -> 14% of each run, Pallas kernels for 0% -> 0%
where the time goes in v1:
time: 571 us; the launch traced here: 561 us
  waiting for transfers between devices  219 us (38%)
  local copies, waits for them, and re-layouts  96.5 us (17%)
  blocking collectives  95.8 us (17%)
  matrix products  49.2 us (9%)
  starting transfers between devices  42.5 us (7%)
  other arithmetic  42.4 us (7%)
  between operations  14.9 us (3%)
    all_to_all x2, blocking collectives, to_experts(): lax.all_to_all(outgoing, 'expert', split_axis=1, concat_axis=1, tiled=True)  67.1 us
    all_to_all x2, waiting for transfers between devices, to_tokens(): lax.all_to_all(outgoing, 'expert', split_axis=1, concat_axis=1, tiled=True)  53.8 us
    reduce_scatter x1, waiting for transfers between devices, per_device(): lax.psum_scatter(partial_out.astype(jnp.bfloat16), 'tensor', scatter_dime...  45.5 us
    all_gather x1, waiting for transfers between devices, per_device(): arrived = lax.all_gather(to_experts(outgoing), 'tensor', axis=3, tiled=True)  36.1 us
    ppermute x2, waiting for transfers between devices, gather_around(): lower.append(lax.ppermute(lower[-1] if lower else value, axis, pairs))  32.8 us
    reduce_scatter x1, waiting for transfers between devices, per_device(): lax.psum_scatter(d_entry_part.astype(jnp.bfloat16), 'tensor', scatter_dim...  26.8 us
    ppermute x1, waiting for transfers between devices, per_device(): down_other = lax.ppermute(w_down, 'dp', DP_SWAP)  22.6 us
    all_to_all x2, starting transfers between devices, to_tokens(): lax.all_to_all(outgoing, 'expert', split_axis=1, concat_axis=1, tiled=True)  18.3 us
  transfers between devices with their start and end apart: 20, of which 10 were waited for; matrix products, arithmetic and copies ran while one was open for 14% of the time, Pallas kernels for 0%

profile of v1, /device:TPU:32, one launch (start us, length us, event | category | flops | bytes accessed | tf_op | source)
XLA Modules:
  0.0 560.5 jit_solution(9266879926142511905)
XLA Ops:
  22.7 3.4 scatter_custom_fusion
  37.5 4.0 gather_fusion.2
  43.6 22.6 %collective-permute-done.3 = bf16[2,352,1024]{2,1,0:T(8,128)(2,1)} collective-permute-done((bf16[2,352,1024]{2,1,0:T(8,128)(2,1)}, bf16[2,352,1024]{2,1,0:T(8,128)(2,1)}, u32[]{:S(2)}, u32[]{:S(2)}) %collective-permute-start.3) | collective-permute-done | bytes 1441824 | tf_op jit(solution)/shard_map/ppermute | solution.py:128
  68.3 36.9 %all_to_all.20 = bf16[2,32,14,512]{3,0,2,1:T(2,128)(2,1)S(1)} all-to-all(bf16[2,32,14,512]{3,0,2,1:T(2,128)(2,1)S(1)} %copy.80), channel_id=1, replica_groups=mesh['dp'=2,'expert'=32,'tensor'=4] {'expert'}, dimensions={1} | all-to-all | bytes 1835008 | tf_op jit(solution)/shard_map/all_to_all | solution.py:35
  111.2 36.1 %all-gather.2.cloned.1.call-done = bf16[2,32,14,2048]{3,1,2,0:T(8,128)(2,1)} async-done(((bf16[2,32,14,512]{3,1,2,0:T(8,128)(2,1)}), bf16[2,32,14,2048]{3,1,2,0:T(8,128)(2,1)}) %all-gather.2.cloned.1.call-update) | async-done | bytes 3670032 | tf_op jit(solution)/shard_map/all_gather | solution.py:173
  162.5 6.8 %convolution_convert_fusion = bf16[2,32,14,2048]{3,1,2,0:T(8,128)(2,1)} fusion(bf16[2,32,14,352]{3,1,2,0:T(8,128)(2,1)S(1)} %multiply_convert_fusion.3, bf16[2,352,1024]{2,1,0:T(8,128)(2,1)} %collective-permute-done.3, bf16[2,352,1024]{2,1,0:T(8,128)(2,1)} %param.17, pred[]{:T(512)S(6)} %eq.46), kind=kOutput, calls=%fused_computation.17 | convolution fusion | flops 1306656768 | bytes 7184385 | tf_op jit(solution)/shard_map/escf,efd->escd/dot_general | solution.py:204
  169.3 45.5 %reduce-scatter.3.cloned.1.call-done = bf16[2,32,14,512]{3,1,2,0:T(8,128)(2,1)} async-done(((bf16[2,32,14,2048]{3,1,2,0:T(8,128)(2,1)}), bf16[2,32,14,512]{3,1,2,0:T(8,128)(2,1)}) %reduce-scatter.3.cloned.1.call-update) | async-done | bytes 917520 | tf_op jit(solution)/shard_map/reduce_scatter | solution.py:207
  217.9 9.1 %all-to-all-start.1 = ((bf16[2,32,14,512]{3,0,2,1:T(2,128)(2,1)}), bf16[2,32,14,512]{3,0,2,1:T(2,128)(2,1)}, u32[]{:S(2)}, u32[]{:S(2)}) async-start(bf16[2,32,14,512]{3,0,2,1:T(2,128)(2,1)} %copy.82), calls=%async_computation.2 | async-start | bytes 1835008 | tf_op jit(solution)/shard_map/all_to_all | solution.py:39
  227.7 3.7 gather_fusion.4
  231.6 18.8 %all-to-all-done.1 = bf16[2,32,14,512]{3,0,2,1:T(2,128)(2,1)} async-done(((bf16[2,32,14,512]{3,0,2,1:T(2,128)(2,1)}), bf16[2,32,14,512]{3,0,2,1:T(2,128)(2,1)}, u32[]{:S(2)}, u32[]{:S(2)}) %all-to-all-start.1) | async-done | bytes 917536 | tf_op jit(solution)/shard_map/all_to_all | solution.py:39
  263.1 4.0 gather_fusion.5
  272.3 30.2 %all_to_all.21 = bf16[2,32,14,512]{3,0,2,1:T(2,128)(2,1)S(1)} all-to-all(bf16[2,32,14,512]{3,0,2,1:T(2,128)(2,1)S(1)} %copy.85), channel_id=1, replica_groups=mesh['dp'=2,'expert'=32,'tensor'=4] {'expert'}, dimensions={1} | all-to-all | bytes 1835008 | tf_op jit(solution)/shard_map/all_to_all | solution.py:35
  307.0 20.7 %collective-permute-done.10 = bf16[2,32,14,512]{3,1,2,0:T(8,128)(2,1)} collective-permute-done((bf16[2,32,14,512]{3,1,2,0:T(8,128)(2,1)}, bf16[2,32,14,512]{3,1,2,0:T(8,128)(2,1)}, u32[]{:S(2)}, u32[]{:S(2)}) %collective-permute-start.10) | collective-permute-done | bytes 917536 | tf_op jit(solution)/shard_map/ppermute | solution.py:25
  327.9 7.9 %maximum_select_fusion = bf16[2,2,2048,352]{2,3,1,0:T(8,128)(2,1)} fusion(bf16[1,2,1024,352]{2,3,1,0:T(8,128)(2,1)} %collective-permute-done.8, bf16[1,1,1024,352]{2,3,1,0:T(8,128)(2,1)} %collective-permute-done.9, bf16[1,1,1024,352]{2,3,1,0:T(8,128)(2,1)} %copy-done.9, bf16[2,2,1024,352]{2,3,1,0:T(8,128)(2,1)} %param.16, pred[]{:T(512)S(6)} %eq.46), kind=kLoop, calls=%fused_computation.11 | loop fusion | flops 49020928 | bytes 11534337 | tf_op jit(solution)/shard_map/jit(_where)/select_n | solution.py:163
  338.9 12.1 %collective-permute-done.11 = bf16[2,32,14,512]{3,1,2,0:T(8,128)(2,1)S(1)} collective-permute-done((bf16[2,32,14,512]{3,1,2,0:T(8,128)(2,1)}, bf16[2,32,14,512]{3,1,2,0:T(8,128)(2,1)S(1)}, u32[]{:S(2)}, u32[]{:S(2)}) %collective-permute-start.11) | collective-permute-done | bytes 917536 | tf_op jit(solution)/shard_map/ppermute | solution.py:25
  351.9 7.6 %pad_maximum_fusion = bf16[4,2,32,14,512]{4,1,3,2,0:T(2,128)(2,1)} fusion(bf16[1,2,32,14,512]{4,1,3,2,0:T(2,128)(2,1)S(1)} %bitcast.179, bf16[1,2,32,14,512]{4,1,3,2,0:T(2,128)(2,1)S(1)} %bitcast.177, bf16[1,2,32,14,512]{4,1,3,2,0:T(2,128)(2,1)S(1)} %bitcast.178, bf16[1,2,32,14,512]{4,1,3,2,0:T(2,128)(2,1)S(1)} %bitcast.180), kind=kLoop, calls=%fused_computation.14 | loop fusion | flops 5505024 | bytes 7340032 | tf_op jit(solution)/shard_map/stack | solution.py:28
  359.5 11.2 %gather_fusion.6 = bf16[4,2,32,14,512]{4,1,3,2,0:T(2,128)(2,1)} fusion(bf16[4,2,32,14,512]{4,1,3,2,0:T(2,128)(2,1)} %pad_maximum_fusion, s32[1024]{0:T(1024)S(1)} %pad_clamp_fusion), kind=kCustom, calls=%fused_computation.6 | custom fusion | bytes 7340048 | tf_op jit(solution)/shard_map/gather | solution.py:30
  370.7 6.6 %copy.91 = bf16[2,32,14,4,512]{4,3,1,2,0:T(4,128)(2,1)} copy(bf16[2,32,14,4,512]{4,0,2,1,3:T(2,128)(2,1)} %bitcast.176) | data formatting | bytes 7340032 | tf_op jit(solution)/shard_map/transpose | solution.py:15
  377.3 7.4 %reshape.311 = bf16[2,32,14,2048]{3,1,2,0:T(8,128)(2,1)} reshape(bf16[2,32,14,4,512]{4,3,1,2,0:T(4,128)(2,1)} %copy.91) | data formatting | bytes 7340032 | tf_op jit(solution)/shard_map/reshape | solution.py:15
  384.7 6.8 %multiply_convert_fusion.2 = (bf16[2,32,14,352]{3,1,2,0:T(8,128)(2,1)S(1)}, bf16[2,32,14,352]{3,1,2,0:T(8,128)(2,1)S(1)}) fusion(f32[1,32,14,352]{3,1,2,0:T(8,128)} %copy-done.13, f32[1,32,14,352]{3,1,2,0:T(8,128)} %copy-done.14, f32[1,32,14,352]{3,1,2,0:T(8,128)} %copy-done.12, f32[1,32,14,352]{3,1,2,0:T(8,128)S(1)} %copy-done.11, ...), kind=kOutput, calls=%fused_computation.34 | convolution fusion | flops 1309552640 | bytes 10338305 | tf_op jit(solution)/shard_map/escd,efd->escf/dot_general | solution.py:223
  391.5 4.4 fusion
  396.0 5.7 %add_convert_fusion = bf16[2,32,14,2048]{3,1,2,0:T(8,128)(2,1)} fusion(f32[2,32,14,2048]{3,1,2,0:T(8,128)S(1)} %fusion, bf16[2,32,14,352]{3,1,2,0:T(8,128)(2,1)S(1)} %get-tuple-element.55, bf16[2,2,2048,352]{2,3,1,0:T(8,128)(2,1)} %maximum_select_fusion), kind=kOutput, calls=%fused_computation.10 | convolution fusion | flops 1295515648 | bytes 14524416 | tf_op jit(solution)/shard_map/escf,edf->escd/dot_general | solution.py:229
  402.8 3.9 convolution_bitcast_fusion.1
  412.5 5.6 collective-permute-start.13
  418.0 26.8 %reduce-scatter.5.cloned.1.call-done = bf16[2,32,14,512]{3,1,2,0:T(8,128)(2,1)} async-done(((bf16[2,32,14,2048]{3,1,2,0:T(8,128)(2,1)}), bf16[2,32,14,512]{3,1,2,0:T(8,128)(2,1)}) %reduce-scatter.5.cloned.1.call-update) | async-done | bytes 917520 | tf_op jit(solution)/shard_map/reduce_scatter | solution.py:235
  447.9 9.2 %all-to-all-start.3 = ((bf16[2,32,14,512]{3,0,2,1:T(2,128)(2,1)}), bf16[2,32,14,512]{3,0,2,1:T(2,128)(2,1)S(1)}, u32[]{:S(2)}, u32[]{:S(2)}) async-start(bf16[2,32,14,512]{3,0,2,1:T(2,128)(2,1)} %copy.92), calls=%async_computation.5 | async-start | bytes 1835008 | tf_op jit(solution)/shard_map/all_to_all | solution.py:39
  457.1 4.0 bitcast_convert_fusion
  465.6 35.0 %all-to-all-done.3 = bf16[2,32,14,512]{3,0,2,1:T(2,128)(2,1)S(1)} async-done(((bf16[2,32,14,512]{3,0,2,1:T(2,128)(2,1)}), bf16[2,32,14,512]{3,0,2,1:T(2,128)(2,1)S(1)}, u32[]{:S(2)}, u32[]{:S(2)}) %all-to-all-start.3) | async-done | bytes 917536 | tf_op jit(solution)/shard_map/all_to_all | solution.py:39
  511.6 15.2 %all-reduce.2 = (f32[128]{0:T(128)S(1)}, f32[128,6]{1,0:T(8,128)S(1)}) all-reduce(f32[128]{0:T(128)S(1)} %multiply_reduce_fusion.2, f32[128,6]{1,0:T(8,128)S(1)} %multiply_reduce_fusion), channel_id=1, replica_groups=mesh['dp'=2,'expert'=32,'tensor'=4] {'tensor'}, use_global_device_ids=true, to_apply=%region_11.12 | all-reduce | flops 896 | bytes 7168 | tf_op jit(solution)/shard_map/psum | solution.py:244
  526.9 13.5 %all_gather.7 = bf16[128,2048]{1,0:T(8,128)(2,1)S(1)} all-gather(bf16[128,512]{1,0:T(8,128)(2,1)S(1)} %subtract_convert_fusion), channel_id=1, replica_groups=mesh['dp'=2,'expert'=32,'tensor'=4] {'tensor'}, dimensions={1}, use_global_device_ids=true | all-gather | bytes 655360 | tf_op jit(solution)/shard_map/all_gather | solution.py:252
  541.9 3.4 add_convert_fusion.2
  545.3 5.7 %add_convert_fusion.1 = bf16[2,2,1024,352]{2,3,0,1:T(8,128)(2,1)S(1)} fusion(bf16[2,2,1024,352]{2,3,0,1:T(8,128)(2,1)} %collective-permute-done.13, pred[]{:T(512)S(6)} %eq.46, bf16[2,2,2048,352]{2,3,0,1:T(8,128)(2,1)} %copy-done.1), kind=kLoop, calls=%fused_computation.13 | loop fusion | flops 7208960 | bytes 11534337 | tf_op jit(solution)/shard_map/convert_element_type | solution.py:100
  (162 shorter events, 112.1 us)
Async XLA Ops:
  7.2 140.1 %all-gather.2.cloned.1.call-start = ((), (), s32[]{:S(2)}) async-start(), calls=%async_computation.6 | async-start | bytes 4587520 | tf_op jit(solution)/shard_map/all_gather | solution.py:173
  8.8 7.9 %copy-start.5 = (bf16[2,2,1024,352]{2,3,1,0:T(8,128)(2,1)S(1)}, bf16[2,2,1024,352]{2,3,1,0:T(8,128)(2,1)}, u32[]{:S(2)}) copy-start(bf16[2,2,1024,352]{2,3,1,0:T(8,128)(2,1)} %param.16) | copy-start | bytes 8650756
  8.8 11.2 %copy-start.22 = (s32[128,6]{0,1:T(8,128)S(1)}, s32[128,6]{0,1:T(8,128)}, u32[]{:S(2)}) copy-start(s32[128,6]{0,1:T(8,128)} %param.15) | copy-start | bytes 9220
  11.0 15.1 %collective-permute-start = (bf16[128,512]{1,0:T(8,128)(2,1)}, bf16[128,512]{1,0:T(8,128)(2,1)}, u32[]{:S(2)}, u32[]{:S(2)}) collective-permute-start(bf16[128,512]{1,0:T(8,128)(2,1)} %get-tuple-element.60), channel_id=1, source_target_pairs={{0,1},{1,2},{2,3},{3,0},{4,5},{5,6},{6,7},{7,4},{8,9},{9,10},{10,1... | collective-permute-start | bytes 393224 | tf_op jit(solution)/shard_map/ppermute | solution.py:46
  12.5 13.6 %collective-permute-start.1 = (bf16[128,512]{1,0:T(8,128)(2,1)}, bf16[128,512]{1,0:T(8,128)(2,1)}, u32[]{:S(2)}, u32[]{:S(2)}) collective-permute-start(bf16[128,512]{1,0:T(8,128)(2,1)} %get-tuple-element.59), channel_id=1, source_target_pairs={{0,2},{1,3},{2,0},{3,1},{4,6},{5,7},{6,4},{7,5},{8,10},{9,11},{10,... | collective-permute-start | bytes 393224 | tf_op jit(solution)/shard_map/ppermute | solution.py:46
  15.3 10.9 %collective-permute-start.2 = (bf16[128,512]{1,0:T(8,128)(2,1)S(1)}, bf16[128,512]{1,0:T(8,128)(2,1)}, u32[]{:S(2)}, u32[]{:S(2)}) collective-permute-start(bf16[128,512]{1,0:T(8,128)(2,1)S(1)} %get-tuple-element.58), channel_id=1, source_target_pairs={{0,3},{1,0},{2,1},{3,2},{4,7},{5,4},{6,5},{7,6},{8,11},{9,8},{10,9... | collective-permute-start | bytes 393224 | tf_op jit(solution)/shard_map/ppermute | solution.py:46
  17.9 25.7 %collective-permute-start.4 = (bf16[1,1,1024,352]{2,3,1,0:T(8,128)(2,1)}, bf16[1,1,1024,352]{2,3,1,0:T(8,128)(2,1)S(1)}, u32[]{:S(2)}, u32[]{:S(2)}) collective-permute-start(bf16[1,1,1024,352]{2,3,1,0:T(8,128)(2,1)} %get-tuple-element.54), channel_id=1, source_target_pairs={{0,128},{128,0},{1,129},{129,1},{2,130},{130,2},{3,131},{131,3},{4... | collective-permute-start | bytes 2162696 | tf_op jit(solution)/shard_map/ppermute | solution.py:154
  18.0 48.1 %collective-permute-start.3 = (bf16[2,352,1024]{2,1,0:T(8,128)(2,1)}, bf16[2,352,1024]{2,1,0:T(8,128)(2,1)}, u32[]{:S(2)}, u32[]{:S(2)}) collective-permute-start(bf16[2,352,1024]{2,1,0:T(8,128)(2,1)} %param.17), channel_id=1, source_target_pairs={{0,128},{128,0},{1,129},{129,1},{2,130},{130,2},{3,131},{131,3},{4... | collective-permute-start | bytes 4325384 | tf_op jit(solution)/shard_map/ppermute | solution.py:128
  30.9 4.8 collective-permute-start.5
  31.6 5.1 collective-permute-start.6
  32.5 4.2 collective-permute-start.7
  43.6 105.9 %copy-start.9 = (bf16[1,1,1024,352]{2,3,1,0:T(8,128)(2,1)}, bf16[1,1,1024,352]{2,3,1,0:T(8,128)(2,1)S(1)}, u32[]{:S(2)}) copy-start(bf16[1,1,1024,352]{2,3,1,0:T(8,128)(2,1)S(1)} %collective-permute-done.4) | copy-start | bytes 2162692
  106.4 108.5 %reduce-scatter.3.cloned.1.call-start = ((), (), s32[]{:S(2)}) async-start(), calls=%async_computation.7 | async-start | bytes 4587520 | tf_op jit(solution)/shard_map/reduce_scatter | solution.py:207
  109.0 44.6 %collective-permute-start.8 = (bf16[1,2,1024,352]{2,3,1,0:T(8,128)(2,1)}, bf16[1,2,1024,352]{2,3,1,0:T(8,128)(2,1)}, u32[]{:S(2)}, u32[]{:S(2)}) collective-permute-start(bf16[1,2,1024,352]{2,3,1,0:T(8,128)(2,1)} %slice.107), channel_id=1, source_target_pairs={{0,128},{128,0},{1,129},{129,1},{2,130},{130,2},{3,131},{131,3},{4... | collective-permute-start | bytes 4325384 | tf_op jit(solution)/shard_map/ppermute | solution.py:159
  109.9 48.7 %collective-permute-start.9 = (bf16[1,1,1024,352]{2,3,1,0:T(8,128)(2,1)}, bf16[1,1,1024,352]{2,3,1,0:T(8,128)(2,1)}, u32[]{:S(2)}, u32[]{:S(2)}) collective-permute-start(bf16[1,1,1024,352]{2,3,1,0:T(8,128)(2,1)} %get-tuple-element.53), channel_id=1, source_target_pairs={{0,128},{128,0},{1,129},{129,1},{2,130},{130,2},{3,131},{131,3},{4... | collective-permute-start | bytes 2162696 | tf_op jit(solution)/shard_map/ppermute | solution.py:158
  147.3 4.2 copy-start.6
  151.5 8.8 %copy-start.10 = (f32[1,32,14,352]{3,1,2,0:T(8,128)}, f32[1,32,14,352]{3,1,2,0:T(8,128)S(1)}, u32[]{:S(2)}) copy-start(f32[1,32,14,352]{3,1,2,0:T(8,128)S(1)} %fusion.8) | copy-start | bytes 1892356
  155.4 4.9 copy-start.12
  169.3 58.1 %copy-start.23 = (f32[128,6]{0,1:T(8,128)S(1)}, f32[128,6]{0,1:T(8,128)}, u32[]{:S(2)}) copy-start(f32[128,6]{0,1:T(8,128)} %param.14) | copy-start | bytes 9220
  217.9 32.4 %all-to-all-start.1 = ((bf16[2,32,14,512]{3,0,2,1:T(2,128)(2,1)}), bf16[2,32,14,512]{3,0,2,1:T(2,128)(2,1)}, u32[]{:S(2)}, u32[]{:S(2)}) async-start(bf16[2,32,14,512]{3,0,2,1:T(2,128)(2,1)} %copy.82), calls=%async_computation.2 | async-start | bytes 1835008 | tf_op jit(solution)/shard_map/all_to_all | solution.py:39
  227.0 217.8 %reduce-scatter.5.cloned.1.call-start = ((), (), s32[]{:S(2)}) async-start(), calls=%async_computation.8 | async-start | bytes 4587520 | tf_op jit(solution)/shard_map/reduce_scatter | solution.py:235
  257.4 4.8 copy-start.21
  303.7 24.0 %collective-permute-start.10 = (bf16[2,32,14,512]{3,1,2,0:T(8,128)(2,1)}, bf16[2,32,14,512]{3,1,2,0:T(8,128)(2,1)}, u32[]{:S(2)}, u32[]{:S(2)}) collective-permute-start(bf16[2,32,14,512]{3,1,2,0:T(8,128)(2,1)} %copy.86), channel_id=1, source_target_pairs={{0,1},{1,2},{2,3},{3,0},{4,5},{5,6},{6,7},{7,4},{8,9},{9,10},{10,1... | collective-permute-start | bytes 2752520 | tf_op jit(solution)/shard_map/ppermute | solution.py:25
  304.0 34.0 %collective-permute-start.12 = (bf16[2,32,14,512]{3,1,2,0:T(8,128)(2,1)}, bf16[2,32,14,512]{3,1,2,0:T(8,128)(2,1)S(1)}, u32[]{:S(2)}, u32[]{:S(2)}) collective-permute-start(bf16[2,32,14,512]{3,1,2,0:T(8,128)(2,1)} %copy.86), channel_id=1, source_target_pairs={{1,0},{2,1},{3,2},{0,3},{5,4},{6,5},{7,6},{4,7},{9,8},{10,9},{11,1... | collective-permute-start | bytes 2752520 | tf_op jit(solution)/shard_map/ppermute | solution.py:27
  327.7 23.2 %collective-permute-start.11 = (bf16[2,32,14,512]{3,1,2,0:T(8,128)(2,1)}, bf16[2,32,14,512]{3,1,2,0:T(8,128)(2,1)S(1)}, u32[]{:S(2)}, u32[]{:S(2)}) collective-permute-start(bf16[2,32,14,512]{3,1,2,0:T(8,128)(2,1)} %collective-permute-done.10), channel_id=1, source_target_pairs={{0,1},{1,2},{2,3},{3,0},{4,5},{5,6},{6,7},{7,4},{8,9},{9,10},{10,1... | collective-permute-start | bytes 2752520 | tf_op jit(solution)/shard_map/ppermute | solution.py:25
  377.3 7.4 %copy-start.11 = (f32[1,32,14,352]{3,1,2,0:T(8,128)S(1)}, f32[1,32,14,352]{3,1,2,0:T(8,128)}, u32[]{:S(2)}) copy-start(f32[1,32,14,352]{3,1,2,0:T(8,128)} %copy-done.10) | copy-start | bytes 1892356
  391.5 4.4 copy-start.19
  391.5 4.4 copy-start.16
  412.5 129.4 %collective-permute-start.13 = (bf16[2,2,1024,352]{2,3,0,1:T(8,128)(2,1)}, bf16[2,2,1024,352]{2,3,0,1:T(8,128)(2,1)}, u32[]{:S(2)}, u32[]{:S(2)}) collective-permute-start(bf16[2,2,1024,352]{2,3,0,1:T(8,128)(2,1)} %broadcast_select_fusion), channel_id=1, source_target_pairs={{0,128},{128,0},{1,129},{129,1},{2,130},{130,2},{3,131},{131,3},{4... | collective-permute-start | bytes 8650760 | tf_op jit(solution)/shard_map/ppermute | solution.py:95
  447.9 52.8 %all-to-all-start.3 = ((bf16[2,32,14,512]{3,0,2,1:T(2,128)(2,1)}), bf16[2,32,14,512]{3,0,2,1:T(2,128)(2,1)S(1)}, u32[]{:S(2)}, u32[]{:S(2)}) async-start(bf16[2,32,14,512]{3,0,2,1:T(2,128)(2,1)} %copy.92), calls=%async_computation.5 | async-start | bytes 1835008 | tf_op jit(solution)/shard_map/all_to_all | solution.py:39
  463.9 78.0 %collective-permute-start.14 = (bf16[2,352,1024]{2,1,0:T(8,128)(2,1)}, bf16[2,352,1024]{2,1,0:T(8,128)(2,1)}, u32[]{:S(2)}, u32[]{:S(2)}) collective-permute-start(bf16[2,352,1024]{2,1,0:T(8,128)(2,1)} %broadcast_select_fusion.1), channel_id=1, source_target_pairs={{0,128},{128,0},{1,129},{129,1},{2,130},{130,2},{3,131},{131,3},{4... | collective-permute-start | bytes 4325384 | tf_op jit(solution)/shard_map/ppermute | solution.py:95
  526.7 15.2 %copy-start.4 = (bf16[2,352,2048]{2,1,0:T(8,128)(2,1)S(1)}, bf16[2,352,2048]{2,1,0:T(8,128)(2,1)}, u32[]{:S(2)}) copy-start(bf16[2,352,2048]{2,1,0:T(8,128)(2,1)} %copy-done.3) | copy-start | bytes 8650756
  (12 other events, 29.2 us)
Sparse Core Ops, SparseCore 0:
  106.5 40.7 all-gather.1
  169.5 45.3 reduce-scatter.2
  401.8 42.9 reduce-scatter.4
